TPU v7x, 128 devices: a whole 4x4x4 slice. The times are simulated.
128 devices in a mesh: owner: 32 (over z, x, core), tensor: 4 (over y).
Axes of the slice: x: 4, y: 4, z: 4, core: 2. Of those that a mesh axis runs over, the one named last changes fastest.
Arguments:
- gradients: bfloat16 [160, 1536, 512], P(None, 'owner', 'tensor'), may hold values from -12 to 12
- moments: bfloat16 [160, 1536, 512], P(None, 'owner', 'tensor'), may hold values from -12 to 12
- stats: float32 [256, 512, 512], P(('owner', 'tensor')), may hold values from -1 to 11, as said below
- bases: float32 [256, 512, 512], P(('owner', 'tensor')), may hold values from -1 to 2
- second: bfloat16 [256, 1536, 512], P(('owner', 'tensor')), may hold values from 0.19921875 to 8
- owner_list: int32 [160], replicated, may hold values from 0 to 127, as said below
Outputs:
- new_moments: bfloat16 [160, 1536, 512], P(None, 'owner', 'tensor')
- update: bfloat16 [160, 1536, 512], P(None, 'owner', 'tensor')
- new_stats: float32 [256, 512, 512], P(('owner', 'tensor'))
- new_bases: float32 [256, 512, 512], P(('owner', 'tensor'))
- new_second: bfloat16 [256, 1536, 512], P(('owner', 'tensor'))
Inputs may be any that keep to these rules, and one draw needn't show every extreme that they name: `owner_list`: no device owns more than 2 matrices, and at least one owns 2. `stats`: Symmetric.
All inputs are finite; a program needn't handle non-finite values.
Results may differ from a plain program's by a relative error of at most 0.0077.
Values may be sent and summed in bfloat16 or wider, within the bound.
No kernel may reach another device: no remote copies, remote signals or barrier semaphores. Data moves between devices by JAX's collectives and lax.ppermute only.
A program may use at most 128 MiB of HBM per device.

v0:
```python
import jax
import jax.numpy as jnp
from jax import lax
from jax.sharding import PartitionSpec as P


def refine(iterate):
    for sweep in range(2):
        iter_b = iterate.astype(jnp.bfloat16)
        square = jnp.einsum(
            "cki,ckj->cij", iter_b, iter_b, preferred_element_type=jnp.float32
        ).astype(jnp.bfloat16)
        iterate = 1.5 * iterate - 0.5 * jnp.einsum(
            "cik,ckj->cij", iter_b, square, preferred_element_type=jnp.float32
        )
    return iterate


def local(gradients, moments, stats, bases, second, owner_list):
    matrices, piece_rows, piece_cols = gradients.shape
    capacity = stats.shape[0]
    owners = lax.axis_size("owner")
    tensors = lax.axis_size("tensor")
    devices = owners * tensors
    myself = lax.axis_index(("owner", "tensor"))
    matrix_ids = jnp.arange(matrices, dtype=jnp.int32)
    shared = owner_list[:, None] == owner_list[None, :]
    earlier = matrix_ids[:, None] < matrix_ids[None, :]
    position = jnp.sum((shared & earlier).astype(jnp.int32), axis=0)
    slot_id = owner_list * capacity + position
    targets = (
        jnp.arange(devices, dtype=jnp.int32)[None, :] * capacity
        + jnp.arange(capacity, dtype=jnp.int32)[:, None]
    )
    selector = (targets[:, :, None] == slot_id[None, None, :]).astype(jnp.bfloat16)
    new_moments = (0.9 * moments.astype(jnp.float32) + 0.1 * gradients.astype(jnp.float32)).astype(
        jnp.bfloat16
    )
    flat_grads = gradients.reshape(matrices, piece_rows * piece_cols)
    flat_moms = new_moments.reshape(matrices, piece_rows * piece_cols)
    send_grads = jnp.einsum(
        "cdn,nk->cdk", selector, flat_grads, preferred_element_type=jnp.float32
    ).astype(jnp.bfloat16)
    send_moms = jnp.einsum(
        "cdn,nk->cdk", selector, flat_moms, preferred_element_type=jnp.float32
    ).astype(jnp.bfloat16)
    got_grads, got_moms = (
        lax.all_to_all(
            send_grads.reshape(capacity, devices, piece_rows, piece_cols),
            ("owner", "tensor"),
            split_axis=1,
            concat_axis=1,
            tiled=True,
        ),
        lax.all_to_all(
            send_moms.reshape(capacity, devices, piece_rows, piece_cols),
            ("owner", "tensor"),
            split_axis=1,
            concat_axis=1,
            tiled=True,
        ),
    )

    def assemble(pieces):
        blocks = pieces.reshape(capacity, owners, tensors, piece_rows, piece_cols)
        return blocks.transpose(0, 1, 3, 2, 4).reshape(
            capacity, owners * piece_rows, tensors * piece_cols
        )

    grad_mats = assemble(got_grads)
    moment_mats = assemble(got_moms)
    full_rows = grad_mats.shape[1]
    full_cols = grad_mats.shape[2]
    gram = jnp.einsum("cri,crj->cij", grad_mats, grad_mats, preferred_element_type=jnp.float32)
    stat_next = 0.95 * stats + 0.05 / full_rows * gram
    basis_b = bases.astype(jnp.bfloat16)
    rotated = jnp.einsum("crk,ckj->crj", grad_mats, basis_b, preferred_element_type=jnp.float32)
    second_next = 0.95 * second.astype(jnp.float32) + 0.05 * rotated * rotated
    moment_rot = jnp.einsum(
        "crk,ckj->crj", moment_mats, basis_b, preferred_element_type=jnp.float32
    )
    scaled = (moment_rot / (jnp.sqrt(second_next) + 1e-06)).astype(jnp.bfloat16)
    step_mats = jnp.einsum(
        "crj,ckj->crk", scaled, basis_b, preferred_element_type=jnp.float32
    ).astype(jnp.bfloat16)
    step_pieces = step_mats.reshape(capacity, owners, piece_rows, tensors, piece_cols).transpose(
        0, 1, 3, 2, 4
    )
    returned = lax.all_to_all(
        step_pieces.reshape(capacity, devices, piece_rows, piece_cols),
        ("owner", "tensor"),
        split_axis=1,
        concat_axis=1,
        tiled=True,
    )
    returned = returned.reshape(capacity, devices, piece_rows * piece_cols)
    update = jnp.einsum(
        "cdn,cdk->nk", selector, returned, preferred_element_type=jnp.float32
    ).astype(jnp.bfloat16)
    update = update.reshape(matrices, piece_rows, piece_cols)
    power = jnp.einsum(
        "cij,cjk->cik",
        stat_next,
        bases,
        precision=lax.Precision.HIGHEST,
        preferred_element_type=jnp.float32,
    )
    iterate = power / (
        2.0 * jnp.sqrt(full_cols * jnp.mean(power * power, axis=(1, 2), keepdims=True) + 1e-06)
    )
    iterate = refine(iterate)
    my_slots = myself * capacity + jnp.arange(capacity, dtype=jnp.int32)
    filled = jnp.any(my_slots[:, None] == slot_id[None, :], axis=1).astype(jnp.float32)[
        :, None, None
    ]
    new_stats = stat_next * filled
    new_bases = iterate * filled
    new_second = (second_next * filled).astype(jnp.bfloat16)
    return (new_moments, update, new_stats, new_bases, new_second)


def solution(mesh):
    placed = (
        P(None, "owner", "tensor"),
        P(None, "owner", "tensor"),
        P(("owner", "tensor"), None, None),
        P(("owner", "tensor"), None, None),
        P(("owner", "tensor"), None, None),
        P(),
    )
    return jax.shard_map(
        local,
        mesh=mesh,
        in_specs=placed,
        out_specs=(
            P(None, "owner", "tensor"),
            P(None, "owner", "tensor"),
            P(("owner", "tensor"), None, None),
            P(("owner", "tensor"), None, None),
            P(("owner", "tensor"), None, None),
        ),
        check_vma=False,
    )
```

profile of v0, /device:TPU:1, one launch (start us, length us, event | category | flops | bytes accessed | tf_op | source)
XLA Modules:
  0.0 206.2 jit_solution(12441411162503713069)
XLA Ops:
  0.6 2.9 %add_convert_fusion = bf16[160,48,128]{2,1,0:T(8,128)(2,1)S(1)} fusion(bf16[160,48,128]{2,1,0:T(8,128)(2,1)} %param.6, bf16[160,48,128]{2,1,0:T(8,128)(2,1)} %param.7), kind=kLoop, calls=%fused_computation.8 | loop fusion | flops 5898240 | bytes 5898240 | tf_op jit(solution)/shard_map/convert_element_type | solution.py:36
  3.6 1.9 reshape.103
  5.5 0.1 convert_reduce_fusion
  5.6 2.6 %convolution_convert_fusion.1 = bf16[2,128,6144]{2,1,0:T(8,128)(2,1)S(1)} fusion(bf16[160,6144,1]{1,0,2:T(8,128)(2,1)} %reshape.103, s32[2,128]{1,0:T(2,128)S(1)} %iota_add_fusion, s32[160]{0:T(256)S(1)} %multiply_add_fusion.1), kind=kOutput, calls=%fused_computation.2 | convolution fusion | flops 504930304 | bytes 5113472 | tf_op jit(solution)/shard_map/cdn,nk->cdk/dot_general | solution.py:44
  8.2 0.7 copy.50
  9.0 2.2 %copy.33 = bf16[2,128,48,128]{3,2,0,1:T(8,128)(2,1)} copy(bf16[2,128,48,128]{3,2,1,0:T(8,128)(2,1)S(1)} %bitcast.42) | data formatting | bytes 6291456 | tf_op jit(solution)/shard_map/reshape | solution.py:56
  11.2 11.5 %all-to-all-start = ((bf16[2,128,48,128]{3,2,0,1:T(8,128)(2,1)}), bf16[2,128,48,128]{3,2,0,1:T(8,128)(2,1)S(1)}, u32[]{:S(2)}, u32[]{:S(2)}) async-start(bf16[2,128,48,128]{3,2,0,1:T(8,128)(2,1)} %copy.33), calls=%async_computation | async-start | bytes 6291456 | tf_op jit(solution)/shard_map/all_to_all | solution.py:55
  22.7 4.0 %reshape.104 = bf16[160,6144,1]{1,0,2:T(8,128)(2,1)} reshape(bf16[160,48,128]{2,1,0:T(8,128)(2,1)} %param.6) | data formatting | bytes 3932160 | tf_op jit(solution)/shard_map/reshape | solution.py:39
  26.6 2.6 %convolution_convert_fusion = bf16[2,128,6144]{2,1,0:T(8,128)(2,1)S(1)} fusion(bf16[160,6144,1]{1,0,2:T(8,128)(2,1)} %reshape.104, s32[2,128]{1,0:T(2,128)S(1)} %iota_add_fusion, s32[160]{0:T(256)S(1)} %multiply_add_fusion.1), kind=kOutput, calls=%fused_computation.1 | convolution fusion | flops 504930304 | bytes 5113472 | tf_op jit(solution)/shard_map/cdn,nk->cdk/dot_general | solution.py:41
  29.3 0.7 copy.51
  30.0 2.2 %copy.36 = bf16[2,128,48,128]{3,2,0,1:T(8,128)(2,1)} copy(bf16[2,128,48,128]{3,2,1,0:T(8,128)(2,1)S(1)} %bitcast.44) | data formatting | bytes 6291456 | tf_op jit(solution)/shard_map/reshape | solution.py:49
  32.2 32.1 %all-to-all-done = bf16[2,128,48,128]{3,2,0,1:T(8,128)(2,1)S(1)} async-done(((bf16[2,128,48,128]{3,2,0,1:T(8,128)(2,1)}), bf16[2,128,48,128]{3,2,0,1:T(8,128)(2,1)S(1)}, u32[]{:S(2)}, u32[]{:S(2)}) %all-to-all-start) | async-done | bytes 3145760 | tf_op jit(solution)/shard_map/all_to_all | solution.py:55
  64.4 4.8 %all-to-all-start.1 = ((bf16[2,128,48,128]{3,2,0,1:T(8,128)(2,1)}), bf16[2,128,48,128]{3,2,0,1:T(8,128)(2,1)}, u32[]{:S(2)}, u32[]{:S(2)}) async-start(bf16[2,128,48,128]{3,2,0,1:T(8,128)(2,1)} %copy.36), calls=%async_computation.1 | async-start | bytes 6291456 | tf_op jit(solution)/shard_map/all_to_all | solution.py:48
  69.2 0.2 compare_reduce_fusion
  69.4 3.3 %copy.35 = bf16[2,32,48,4,128]{4,3,2,1,0:T(4,128)(2,1)} copy(bf16[2,32,48,4,128]{4,2,0,3,1:T(8,128)(2,1)S(1)} %bitcast.39) | data formatting | bytes 6291456 | tf_op jit(solution)/shard_map/transpose | solution.py:66
  72.7 5.7 %reshape.94 = bf16[2,1536,512]{2,1,0:T(8,128)(2,1)} reshape(bf16[2,32,48,4,128]{4,3,2,1,0:T(4,128)(2,1)} %copy.35) | data formatting | bytes 6291456 | tf_op jit(solution)/shard_map/reshape | solution.py:66
  78.4 32.1 %all-to-all-done.1 = bf16[2,128,48,128]{3,2,0,1:T(8,128)(2,1)} async-done(((bf16[2,128,48,128]{3,2,0,1:T(8,128)(2,1)}), bf16[2,128,48,128]{3,2,0,1:T(8,128)(2,1)}, u32[]{:S(2)}, u32[]{:S(2)}) %all-to-all-start.1) | async-done | bytes 3145760 | tf_op jit(solution)/shard_map/all_to_all | solution.py:48
  110.5 5.2 %copy.58 = bf16[2,32,4,48,128]{4,2,3,1,0:T(4,128)(2,1)} copy(bf16[2,32,4,48,128]{4,3,0,2,1:T(8,128)(2,1)} %bitcast.3) | data formatting | bytes 6291456 | tf_op jit(solution)/shard_map/reshape | solution.py:65
  115.7 4.0 %reshape.98 = bf16[2,1536,512]{2,1,0:T(8,128)(2,1)S(1)} reshape(bf16[2,32,48,4,128]{4,3,2,1,0:T(4,128)(2,1)} %bitcast.45) | data formatting | bytes 6291456 | tf_op jit(solution)/shard_map/reshape | solution.py:66
  119.7 8.5 %multiply_convert_fusion = (bf16[2,1536,512]{2,1,0:T(8,128)(2,1)}, f32[2,1536,512]{2,1,0:T(8,128)}) fusion(bf16[2,1536,512]{2,1,0:T(8,128)(2,1)} %param.10, f32[2]{0:T(128)S(1)} %convert_element_type.67, bf16[2,1536,512]{2,1,0:T(8,128)(2,1)S(1)} %reshape.98, f32[2,512,512]{2,1,0:T(8,128)} %param.9), kind=kOutput, calls=%fused_computation.6 | convolution fusion | flops 1622147072 | bytes 17825800 | tf_op jit(solution)/shard_map/crk,ckj->crj/dot_general | solution.py:77
  128.2 12.4 %convolution_convert_fusion.2 = bf16[2,1536,512]{2,1,0:T(8,128)(2,1)} fusion(bf16[2,1536,512]{2,1,0:T(8,128)(2,1)} %reshape.94, f32[2,1536,512]{2,1,0:T(8,128)} %get-tuple-element.10, bf16[2,1536,512]{2,1,0:T(8,128)(2,1)} %param.10, f32[2,512,512]{2,1,0:T(8,128)} %param.9), kind=kOutput, calls=%fused_computation.9 | convolution fusion | flops 3236429824 | bytes 17825792 | tf_op jit(solution)/shard_map/crj,ckj->crk/dot_general | solution.py:83
  140.6 5.5 %reshape.99 = bf16[2,32,48,4,128]{4,3,2,1,0:T(4,128)(2,1)} reshape(bf16[2,1536,512]{2,1,0:T(8,128)(2,1)} %convolution_convert_fusion.2) | data formatting | bytes 6291456 | tf_op jit(solution)/shard_map/reshape | solution.py:86
  146.1 4.2 %copy.48 = bf16[2,32,48,4,128]{4,2,0,3,1:T(8,128)(2,1)} copy(bf16[2,32,48,4,128]{4,3,2,1,0:T(4,128)(2,1)} %reshape.99) | data formatting | bytes 6291456 | tf_op jit(solution)/shard_map/reshape | solution.py:90
  150.3 4.9 %all-to-all-start.2 = ((bf16[2,128,48,128]{3,2,0,1:T(8,128)(2,1)}), bf16[2,128,48,128]{3,2,0,1:T(8,128)(2,1)}, u32[]{:S(2)}, u32[]{:S(2)}) async-start(bf16[2,128,48,128]{3,2,0,1:T(8,128)(2,1)} %bitcast.40), calls=%async_computation.2 | async-start | bytes 6291456 | tf_op jit(solution)/shard_map/all_to_all | solution.py:89
  155.2 5.0 %broadcast_multiply_fusion = (f32[2,512,512]{2,1,0:T(8,128)}, f32[2,512,512]{2,1,0:T(8,128)S(1)}) fusion(f32[2]{0:T(128)S(1)} %convert_element_type.67, bf16[2,1536,512]{2,1,0:T(8,128)(2,1)S(1)} %reshape.98, f32[2,512,512]{2,1,0:T(8,128)} %param.8), kind=kOutput, calls=%fused_computation.23 | convolution fusion | flops 1612709888 | bytes 9437192 | tf_op jit(solution)/shard_map/cri,crj->cij/dot_general | solution.py:74
  160.2 3.7 %multiply_reduce_fusion = (f32[2]{0:T(128)S(1)}, f32[2,512,512]{2,1,0:T(8,128)S(1)}) fusion(f32[2,512,512]{2,1,0:T(8,128)S(1)} %get-tuple-element.6, f32[2,512,512]{2,1,0:T(8,128)S(1)} %copy-done), kind=kOutput, calls=%fused_computation.14 | convolution fusion | flops 3222274048 | bytes 6291464 | tf_op jit(solution)/shard_map/cij,cjk->cik/dot_general | solution.py:101
  163.9 2.8 %multiply_subtract_fusion = f32[2,512,512]{2,1,0:T(8,128)} fusion(f32[2,512,512]{2,1,0:T(8,128)S(1)} %get-tuple-element.8, f32[2]{0:T(128)S(1)} %sqrt_multiply_fusion), kind=kOutput, calls=%fused_computation.13 | convolution fusion | flops 1078460416 | bytes 4194312 | tf_op jit(solution)/shard_map/cik,ckj->cij/dot_general | solution.py:13
  166.7 6.3 %subtract_multiply_fusion = f32[2,512,512]{2,1,0:T(8,128)} fusion(f32[2,512,512]{2,1,0:T(8,128)} %multiply_subtract_fusion, f32[2]{0:T(128)S(1)} %convert_element_type.67), kind=kOutput, calls=%fused_computation.12 | convolution fusion | flops 1077411840 | bytes 4194312 | tf_op jit(solution)/shard_map/cik,ckj->cij/dot_general | solution.py:13
  173.1 23.4 %all-to-all-done.2 = bf16[2,128,48,128]{3,2,0,1:T(8,128)(2,1)} async-done(((bf16[2,128,48,128]{3,2,0,1:T(8,128)(2,1)}), bf16[2,128,48,128]{3,2,0,1:T(8,128)(2,1)}, u32[]{:S(2)}, u32[]{:S(2)}) %all-to-all-start.2) | async-done | bytes 3145760 | tf_op jit(solution)/shard_map/all_to_all | solution.py:89
  196.4 6.0 %reshape.108 = bf16[2,128,6144]{2,0,1:T(2,128)(2,1)S(1)} reshape(bf16[2,128,48,128]{3,2,0,1:T(8,128)(2,1)} %all-to-all-done.2) | data formatting | bytes 6291456 | tf_op jit(solution)/shard_map/reshape | solution.py:96
  202.4 2.1 %fusion.3 = bf16[20,8,48,128]{3,1,2,0:T(8,128)(2,1)S(1)} fusion(bf16[2,128,6144]{2,0,1:T(2,128)(2,1)S(1)} %reshape.108, s32[2,128]{1,0:T(2,128)S(1)} %iota_add_fusion, s32[160]{0:T(256)S(1)} %multiply_add_fusion.1), kind=kOutput, calls=%fused_computation.16 | convolution fusion | flops 504340480 | bytes 5113472 | tf_op jit(solution)/shard_map/cdn,cdk->nk/dot_general | solution.py:97
  204.5 1.7 copy.52
  (12 shorter events, 0.1 us)
Async XLA Ops:
  3.5 4.7 %copy-start.1 = (bf16[160,48,128]{2,1,0:T(8,128)(2,1)}, bf16[160,48,128]{2,1,0:T(8,128)(2,1)S(1)}, u32[]{:S(2)}) copy-start(bf16[160,48,128]{2,1,0:T(8,128)(2,1)S(1)} %add_convert_fusion) | copy-start | bytes 5898244
  3.6 1.9 copy-start.2
  11.2 53.2 %all-to-all-start = ((bf16[2,128,48,128]{3,2,0,1:T(8,128)(2,1)}), bf16[2,128,48,128]{3,2,0,1:T(8,128)(2,1)S(1)}, u32[]{:S(2)}, u32[]{:S(2)}) async-start(bf16[2,128,48,128]{3,2,0,1:T(8,128)(2,1)} %copy.33), calls=%async_computation | async-start | bytes 6291456 | tf_op jit(solution)/shard_map/all_to_all | solution.py:55
  64.4 46.2 %all-to-all-start.1 = ((bf16[2,128,48,128]{3,2,0,1:T(8,128)(2,1)}), bf16[2,128,48,128]{3,2,0,1:T(8,128)(2,1)}, u32[]{:S(2)}, u32[]{:S(2)}) async-start(bf16[2,128,48,128]{3,2,0,1:T(8,128)(2,1)} %copy.36), calls=%async_computation.1 | async-start | bytes 6291456 | tf_op jit(solution)/shard_map/all_to_all | solution.py:48
  150.3 46.1 %all-to-all-start.2 = ((bf16[2,128,48,128]{3,2,0,1:T(8,128)(2,1)}), bf16[2,128,48,128]{3,2,0,1:T(8,128)(2,1)}, u32[]{:S(2)}, u32[]{:S(2)}) async-start(bf16[2,128,48,128]{3,2,0,1:T(8,128)(2,1)} %bitcast.40), calls=%async_computation.2 | async-start | bytes 6291456 | tf_op jit(solution)/shard_map/all_to_all | solution.py:89
  155.2 5.0 %copy-start = (f32[2,512,512]{2,1,0:T(8,128)S(1)}, f32[2,512,512]{2,1,0:T(8,128)}, u32[]{:S(2)}) copy-start(f32[2,512,512]{2,1,0:T(8,128)} %param.9) | copy-start | bytes 6291460
where the time goes:
time: 207 us; the launch traced here: 206 us
  waiting for transfers between devices  87.6 us (42%)
  local copies, waits for them, and re-layouts  47.3 us (23%)
  matrix products  46.2 us (22%)
  starting transfers between devices  21.2 us (10%)
  other arithmetic  3.23 us (2%)
    all_to_all x1, waiting for transfers between devices, local(): lax.all_to_all(send_moms.reshape(capacity, devices, piece_rows, piece_col...  32.1 us
    all_to_all x1, waiting for transfers between devices, local(): lax.all_to_all(send_grads.reshape(capacity, devices, piece_rows, piece_co...  32.1 us
    all_to_all x1, waiting for transfers between devices, local(): lax.all_to_all(step_pieces.reshape(capacity, devices, piece_rows, piece_c...  23.4 us
    dot_general x1, matrix products, local(): jnp.einsum('crj,ckj->crk', scaled, basis_b, preferred_element_type=jnp.fl...  12.4 us
    all_to_all x1, starting transfers between devices, local(): lax.all_to_all(send_moms.reshape(capacity, devices, piece_rows, piece_col...  11.5 us
    reshape x2, local copies, waits for them, and re-layouts, assemble(): blocks.transpose(0, 1, 3, 2, 4)  9.76 us
    dot_general x2, matrix products, refine(): jnp.einsum('cik,ckj->cij', iter_b, square, preferred_element_type=jnp.flo...  9.13 us
    dot_general x1, matrix products, local(): jnp.einsum('crk,ckj->crj', grad_mats, basis_b, preferred_element_type=jnp...  8.48 us
  transfers between devices with their start and end apart: 3, of which 3 were waited for; matrix products, arithmetic and copies ran while one was open for 18% of the time, Pallas kernels for 0%

commit v1 on v0

--- a/solution.py
+++ b/solution.py
@@ -45,12 +45,20 @@
         "cdn,nk->cdk", selector, flat_moms, preferred_element_type=jnp.float32
     ).astype(jnp.bfloat16)
     got_grads, got_moms = (
-        lax.all_to_all(
-            send_grads.reshape(capacity, devices, piece_rows, piece_cols),
-            ("owner", "tensor"),
-            split_axis=1,
-            concat_axis=1,
-            tiled=True,
+        jnp.concatenate(
+            lax.all_to_all(
+                jnp.stack(
+                    jnp.split(
+                        send_grads.reshape(capacity, devices, piece_rows, piece_cols),
+                        lax.axis_size(("owner", "tensor")),
+                        axis=1,
+                    )
+                ),
+                ("owner", "tensor"),
+                0,
+                0,
+            ),
+            axis=1,
         ),
         lax.all_to_all(
             send_moms.reshape(capacity, devices, piece_rows, piece_cols),

time: 207 us -> 256 us (1.24)
  local copies, waits for them, and re-layouts: 47.3 us -> 123 us
  waiting for transfers between devices: 87.6 us -> 55.5 us
  starting transfers between devices: 21.2 us -> 26.5 us
    unnamed x9 -> x136, local copies, waits for them, and re-layouts: 3.15 us -> 80.1 us
    all_to_all x1, waiting for transfers between devices: 32.1 us -> 0.01 us  [local(): lax.all_to_all(send_moms.reshape(capacity, devices, piece_rows, piece_col...]
    reshape x2 -> x0, local copies, waits for them, and re-layouts: 7.38 us -> none  [the longest x1 5.17 us: assemble(): blocks = pieces.reshape(capacity, owners, tensors, piece_rows, piece_cols)]
    another operation x0 -> x2, local copies, waits for them, and re-layouts: none -> 5.77 us  [the longest x1 5.17 us: assemble(): blocks = pieces.reshape(capacity, owners, tensors, piece_rows, piece_cols)]
    all_to_all x1, starting transfers between devices: 4.85 us -> 10.2 us  [local(): lax.all_to_all(jnp.stack(jnp.split(send_grads.reshape(capacity, devices,...]
  transfers between devices with their start and end apart: 3 -> 3, of which waited for: 3 -> 2; matrix products, arithmetic and copies ran while one was open for 18% -> 44% of each run, Pallas kernels for 0% -> 0%
where the time goes in v1:
time: 256 us; the launch traced here: 255 us
  local copies, waits for them, and re-layouts  123 us (48%)
  waiting for transfers between devices  55.5 us (22%)
  matrix products  46.2 us (18%)
  starting transfers between devices  26.5 us (10%)
  other arithmetic  3.23 us (1%)
    unnamed x136, local copies, waits for them, and re-layouts  80.1 us
    all_to_all x1, waiting for transfers between devices, local(): lax.all_to_all(jnp.stack(jnp.split(send_grads.reshape(capacity, devices,...  32.1 us
    all_to_all x1, waiting for transfers between devices, local(): lax.all_to_all(step_pieces.reshape(capacity, devices, piece_rows, piece_c...  23.3 us
    dot_general x1, matrix products, local(): jnp.einsum('crj,ckj->crk', scaled, basis_b, preferred_element_type=jnp.fl...  12.4 us
    all_to_all x1, starting transfers between devices, local(): lax.all_to_all(send_moms.reshape(capacity, devices, piece_rows, piece_col...  11.5 us
    all_to_all x1, starting transfers between devices, local(): lax.all_to_all(jnp.stack(jnp.split(send_grads.reshape(capacity, devices,...  10.2 us
    reshape x2, local copies, waits for them, and re-layouts, assemble(): blocks.transpose(0, 1, 3, 2, 4)  9.76 us
    dot_general x2, matrix products, refine(): jnp.einsum('cik,ckj->cij', iter_b, square, preferred_element_type=jnp.flo...  9.13 us
  transfers between devices with their start and end apart: 3, of which 2 were waited for; matrix products, arithmetic and copies ran while one was open for 44% of the time, Pallas kernels for 0%

profile of v1, /device:TPU:1, one launch (start us, length us, event | category | flops | bytes accessed | tf_op | source)
XLA Modules:
  0.0 254.9 jit_solution(9153397402286933319)
XLA Ops:
  0.6 2.9 %add_convert_fusion = bf16[160,48,128]{2,1,0:T(8,128)(2,1)S(1)} fusion(bf16[160,48,128]{2,1,0:T(8,128)(2,1)} %param.6, bf16[160,48,128]{2,1,0:T(8,128)(2,1)} %param.7), kind=kLoop, calls=%fused_computation.8 | loop fusion | flops 5898240 | bytes 5898240 | tf_op jit(solution)/shard_map/convert_element_type | solution.py:36
  3.6 1.9 reshape.103
  5.6 2.6 %convolution_convert_fusion.1 = bf16[2,128,6144]{2,1,0:T(8,128)(2,1)S(1)} fusion(bf16[160,6144,1]{1,0,2:T(8,128)(2,1)} %reshape.103, s32[2,128]{1,0:T(2,128)S(1)} %iota_add_fusion, s32[160]{0:T(256)S(1)} %multiply_add_fusion.1), kind=kOutput, calls=%fused_computation.2 | convolution fusion | flops 504930304 | bytes 5113472 | tf_op jit(solution)/shard_map/cdn,nk->cdk/dot_general | solution.py:44
  8.2 0.7 copy.810
  9.0 2.2 copy.540
  11.2 11.5 %all-to-all-start = ((bf16[2,128,48,128]{3,2,0,1:T(8,128)(2,1)}), bf16[2,128,48,128]{3,2,0,1:T(8,128)(2,1)S(1)}, u32[]{:S(2)}, u32[]{:S(2)}) async-start(bf16[2,128,48,128]{3,2,0,1:T(8,128)(2,1)} %copy.540), calls=%async_computation | async-start | bytes 6291456 | tf_op jit(solution)/shard_map/all_to_all | solution.py:63
  22.7 4.0 %reshape.104 = bf16[160,6144,1]{1,0,2:T(8,128)(2,1)} reshape(bf16[160,48,128]{2,1,0:T(8,128)(2,1)} %param.6) | data formatting | bytes 3932160 | tf_op jit(solution)/shard_map/reshape | solution.py:39
  26.6 2.6 %convolution_convert_fusion = bf16[2,128,6144]{2,1,0:T(8,128)(2,1)S(1)} fusion(bf16[160,6144,1]{1,0,2:T(8,128)(2,1)} %reshape.104, s32[2,128]{1,0:T(2,128)S(1)} %iota_add_fusion, s32[160]{0:T(256)S(1)} %multiply_add_fusion.1), kind=kOutput, calls=%fused_computation.1 | convolution fusion | flops 504930304 | bytes 5113472 | tf_op jit(solution)/shard_map/cdn,nk->cdk/dot_general | solution.py:41
  29.3 0.7 copy.811
  54.8 0.6 constant_dynamic-update-slice_fusion.86
  77.2 0.6 constant_dynamic-update-slice_fusion.49
  89.4 0.6 constant_dynamic-update-slice_fusion.29
  100.9 0.6 constant_dynamic-update-slice_fusion.10
  107.6 10.2 %all-to-all-start.1 = ((bf16[128,2,1,48,128]{4,3,1,2,0:T(8,128)(2,1)}), bf16[128,2,1,48,128]{4,3,1,2,0:T(8,128)(2,1)}, u32[]{:S(2)}, u32[]{:S(2)}) async-start(bf16[128,2,1,48,128]{4,3,1,2,0:T(8,128)(2,1)} %constant_dynamic-update-slice_fusion), calls=%async_computation.1 | async-start | bytes 6291456 | tf_op jit(solution)/shard_map/all_to_all | solution.py:49
  118.0 3.3 %copy.542 = bf16[2,32,48,4,128]{4,3,2,1,0:T(4,128)(2,1)} copy(bf16[2,32,48,4,128]{4,2,0,3,1:T(8,128)(2,1)S(1)} %bitcast.935) | data formatting | bytes 6291456 | tf_op jit(solution)/shard_map/transpose | solution.py:74
  121.3 5.7 %reshape.94 = bf16[2,1536,512]{2,1,0:T(8,128)(2,1)} reshape(bf16[2,32,48,4,128]{4,3,2,1,0:T(4,128)(2,1)} %copy.542) | data formatting | bytes 6291456 | tf_op jit(solution)/shard_map/reshape | solution.py:74
  127.0 32.1 %all-to-all-done.1 = bf16[128,2,1,48,128]{4,3,1,2,0:T(8,128)(2,1)} async-done(((bf16[128,2,1,48,128]{4,3,1,2,0:T(8,128)(2,1)}), bf16[128,2,1,48,128]{4,3,1,2,0:T(8,128)(2,1)}, u32[]{:S(2)}, u32[]{:S(2)}) %all-to-all-start.1) | async-done | bytes 3145760 | tf_op jit(solution)/shard_map/all_to_all | solution.py:49
  159.2 5.2 %copy.818 = bf16[2,32,4,48,128]{4,2,3,1,0:T(4,128)(2,1)} copy(bf16[2,32,4,48,128]{4,3,0,2,1:T(8,128)(2,1)} %bitcast.132) | data formatting | bytes 6291456 | tf_op jit(solution)/shard_map/reshape;reshape | solution.py:73
  164.3 4.0 %reshape.98 = bf16[2,1536,512]{2,1,0:T(8,128)(2,1)S(1)} reshape(bf16[2,32,48,4,128]{4,3,2,1,0:T(4,128)(2,1)} %bitcast.940) | data formatting | bytes 6291456 | tf_op jit(solution)/shard_map/reshape | solution.py:74
  168.4 8.5 %multiply_convert_fusion = (bf16[2,1536,512]{2,1,0:T(8,128)(2,1)}, f32[2,1536,512]{2,1,0:T(8,128)}) fusion(bf16[2,1536,512]{2,1,0:T(8,128)(2,1)} %param.10, f32[2]{0:T(128)S(1)} %convert_element_type.67, bf16[2,1536,512]{2,1,0:T(8,128)(2,1)S(1)} %reshape.98, f32[2,512,512]{2,1,0:T(8,128)} %param.9), kind=kOutput, calls=%fused_computation.6 | convolution fusion | flops 1622147072 | bytes 17825800 | tf_op jit(solution)/shard_map/crk,ckj->crj/dot_general | solution.py:85
  176.9 12.4 %convolution_convert_fusion.2 = bf16[2,1536,512]{2,1,0:T(8,128)(2,1)} fusion(bf16[2,1536,512]{2,1,0:T(8,128)(2,1)} %reshape.94, f32[2,1536,512]{2,1,0:T(8,128)} %get-tuple-element.10, bf16[2,1536,512]{2,1,0:T(8,128)(2,1)} %param.10, f32[2,512,512]{2,1,0:T(8,128)} %param.9), kind=kOutput, calls=%fused_computation.9 | convolution fusion | flops 3236429824 | bytes 17825792 | tf_op jit(solution)/shard_map/crj,ckj->crk/dot_general | solution.py:91
  189.3 5.5 %reshape.99 = bf16[2,32,48,4,128]{4,3,2,1,0:T(4,128)(2,1)} reshape(bf16[2,1536,512]{2,1,0:T(8,128)(2,1)} %convolution_convert_fusion.2) | data formatting | bytes 6291456 | tf_op jit(solution)/shard_map/reshape | solution.py:94
  194.8 4.2 %copy.681 = bf16[2,32,48,4,128]{4,2,0,3,1:T(8,128)(2,1)} copy(bf16[2,32,48,4,128]{4,3,2,1,0:T(4,128)(2,1)} %reshape.99) | data formatting | bytes 6291456 | tf_op jit(solution)/shard_map/reshape | solution.py:98
  198.9 4.9 %all-to-all-start.2 = ((bf16[2,128,48,128]{3,2,0,1:T(8,128)(2,1)}), bf16[2,128,48,128]{3,2,0,1:T(8,128)(2,1)}, u32[]{:S(2)}, u32[]{:S(2)}) async-start(bf16[2,128,48,128]{3,2,0,1:T(8,128)(2,1)} %bitcast.936), calls=%async_computation.2 | async-start | bytes 6291456 | tf_op jit(solution)/shard_map/all_to_all | solution.py:97
  203.8 5.0 %broadcast_multiply_fusion = (f32[2,512,512]{2,1,0:T(8,128)}, f32[2,512,512]{2,1,0:T(8,128)S(1)}) fusion(f32[2]{0:T(128)S(1)} %convert_element_type.67, bf16[2,1536,512]{2,1,0:T(8,128)(2,1)S(1)} %reshape.98, f32[2,512,512]{2,1,0:T(8,128)} %param.8), kind=kOutput, calls=%fused_computation.23 | convolution fusion | flops 1612709888 | bytes 9437192 | tf_op jit(solution)/shard_map/cri,crj->cij/dot_general | solution.py:82
  208.9 3.7 %multiply_reduce_fusion = (f32[2]{0:T(128)S(1)}, f32[2,512,512]{2,1,0:T(8,128)S(1)}) fusion(f32[2,512,512]{2,1,0:T(8,128)S(1)} %get-tuple-element.6, f32[2,512,512]{2,1,0:T(8,128)S(1)} %copy-done), kind=kOutput, calls=%fused_computation.14 | convolution fusion | flops 3222274048 | bytes 6291464 | tf_op jit(solution)/shard_map/cij,cjk->cik/dot_general | solution.py:109
  212.6 2.8 %multiply_subtract_fusion = f32[2,512,512]{2,1,0:T(8,128)} fusion(f32[2,512,512]{2,1,0:T(8,128)S(1)} %get-tuple-element.8, f32[2]{0:T(128)S(1)} %sqrt_multiply_fusion), kind=kOutput, calls=%fused_computation.13 | convolution fusion | flops 1078460416 | bytes 4194312 | tf_op jit(solution)/shard_map/cik,ckj->cij/dot_general | solution.py:13
  215.4 6.3 %subtract_multiply_fusion = f32[2,512,512]{2,1,0:T(8,128)} fusion(f32[2,512,512]{2,1,0:T(8,128)} %multiply_subtract_fusion, f32[2]{0:T(128)S(1)} %convert_element_type.67), kind=kOutput, calls=%fused_computation.12 | convolution fusion | flops 1077411840 | bytes 4194312 | tf_op jit(solution)/shard_map/cik,ckj->cij/dot_general | solution.py:13
  221.7 23.3 %all-to-all-done.2 = bf16[2,128,48,128]{3,2,0,1:T(8,128)(2,1)} async-done(((bf16[2,128,48,128]{3,2,0,1:T(8,128)(2,1)}), bf16[2,128,48,128]{3,2,0,1:T(8,128)(2,1)}, u32[]{:S(2)}, u32[]{:S(2)}) %all-to-all-start.2) | async-done | bytes 3145760 | tf_op jit(solution)/shard_map/all_to_all | solution.py:97
  245.1 6.0 %reshape.108 = bf16[2,128,6144]{2,0,1:T(2,128)(2,1)S(1)} reshape(bf16[2,128,48,128]{3,2,0,1:T(8,128)(2,1)} %all-to-all-done.2) | data formatting | bytes 6291456 | tf_op jit(solution)/shard_map/reshape | solution.py:104
  251.1 2.1 fusion.3
  253.2 1.7 copy.812
  (139 shorter events, 75.4 us)
Async XLA Ops:
  3.5 4.7 %copy-start.1 = (bf16[160,48,128]{2,1,0:T(8,128)(2,1)}, bf16[160,48,128]{2,1,0:T(8,128)(2,1)S(1)}, u32[]{:S(2)}) copy-start(bf16[160,48,128]{2,1,0:T(8,128)(2,1)S(1)} %add_convert_fusion) | copy-start | bytes 5898244
  3.6 1.9 copy-start.2
  11.2 96.4 %all-to-all-start = ((bf16[2,128,48,128]{3,2,0,1:T(8,128)(2,1)}), bf16[2,128,48,128]{3,2,0,1:T(8,128)(2,1)S(1)}, u32[]{:S(2)}, u32[]{:S(2)}) async-start(bf16[2,128,48,128]{3,2,0,1:T(8,128)(2,1)} %copy.540), calls=%async_computation | async-start | bytes 6291456 | tf_op jit(solution)/shard_map/all_to_all | solution.py:63
  107.6 51.6 %all-to-all-start.1 = ((bf16[128,2,1,48,128]{4,3,1,2,0:T(8,128)(2,1)}), bf16[128,2,1,48,128]{4,3,1,2,0:T(8,128)(2,1)}, u32[]{:S(2)}, u32[]{:S(2)}) async-start(bf16[128,2,1,48,128]{4,3,1,2,0:T(8,128)(2,1)} %constant_dynamic-update-slice_fusion), calls=%async_computation.1 | async-start | bytes 6291456 | tf_op jit(solution)/shard_map/all_to_all | solution.py:49
  198.9 46.1 %all-to-all-start.2 = ((bf16[2,128,48,128]{3,2,0,1:T(8,128)(2,1)}), bf16[2,128,48,128]{3,2,0,1:T(8,128)(2,1)}, u32[]{:S(2)}, u32[]{:S(2)}) async-start(bf16[2,128,48,128]{3,2,0,1:T(8,128)(2,1)} %bitcast.936), calls=%async_computation.2 | async-start | bytes 6291456 | tf_op jit(solution)/shard_map/all_to_all | solution.py:97
  203.8 5.0 %copy-start = (f32[2,512,512]{2,1,0:T(8,128)S(1)}, f32[2,512,512]{2,1,0:T(8,128)}, u32[]{:S(2)}) copy-start(f32[2,512,512]{2,1,0:T(8,128)} %param.9) | copy-start | bytes 6291460
